TPU v7x, 32 devices: a whole 2x2x4 slice. The times are simulated.
32 devices in a mesh: ta: 8 (over z, y), col: 4 (over x, core).
Axes of the slice: x: 2, y: 2, z: 4, core: 2. Of those that a mesh axis runs over, the one named last changes fastest.
Arguments:
- strain: bfloat16 [2048, 512], P('col', 'ta'), may hold values from -6 to 6
- filter_taps: float32 [64], replicated, may hold values from -0.75 to 0.75
Outputs:
- cross_spectra: bfloat16 [4, 512, 128, 256], P('col', 'ta')
All inputs are finite; a program needn't handle non-finite values.
Results may differ from a plain program's by a relative error of at most 0.0066.
Values may be sent and summed in bfloat16 or wider, within the bound.
No kernel may reach another device: no remote copies, remote signals or barrier semaphores. Data moves between devices by JAX's collectives and lax.ppermute only.
A program may use at most 64 MiB of HBM per device.

v0:
```python
import jax
import jax.numpy as jnp
from jax import lax
from jax.sharding import PartitionSpec as P

NFFT = 256
NF = 128
LAGS = 128


def shifted(block, axis, distance):
    devices = range(lax.axis_size(axis))
    route = [((i - distance) % len(devices), i) for i in devices]
    return lax.ppermute(block, axis, route)


def from_behind(block, axis, distance):
    devices = range(lax.axis_size(axis))
    route = [(i - distance, i) for i in devices if i - distance in devices]
    return lax.ppermute(block, axis, route)


def tap_rows(filter_taps, outputs):
    tap_count = filter_taps.shape[0]
    window = 2 * outputs + tap_count
    flipped = filter_taps[::-1]
    period = jnp.concatenate([flipped, jnp.zeros((window + 2 - tap_count,), jnp.float32)])
    repeated = jnp.tile(period, outputs)[: outputs * window]
    return repeated.reshape(outputs, window)


def decimate(history, samples, filter_taps):
    channels, length = samples.shape
    tap_count = filter_taps.shape[0]
    outputs = min(length, NFFT) // 2
    blocks = length // (2 * outputs)
    joined = jnp.concatenate(
        [history, samples, jnp.zeros((channels, 2 * outputs - tap_count), jnp.float32)], axis=1
    )
    joined = joined.reshape(channels, blocks + 1, 2 * outputs)
    windows = jnp.concatenate([joined[:, :-1], joined[:, 1:, :tap_count]], axis=2)
    matrix = tap_rows(filter_taps, outputs)
    result = jnp.einsum("cbw,tw->cbt", windows, matrix, precision=lax.Precision.HIGHEST)
    return result.reshape(channels, blocks * outputs).astype(jnp.bfloat16)


def fourier_table():
    moment = lax.broadcasted_iota(jnp.int32, (NFFT, NF), 0)
    frequency = lax.broadcasted_iota(jnp.int32, (NFFT, NF), 1) + 1
    phase_index = moment * frequency % NFFT
    angles = phase_index.astype(jnp.float32) * (2.0 * jnp.pi / NFFT)
    window_taper = 0.5 - 0.5 * jnp.cos(moment.astype(jnp.float32) * (2.0 * jnp.pi / NFFT))
    return jnp.concatenate(
        [window_taper * jnp.cos(angles), -window_taper * jnp.sin(angles)], axis=1
    )


def whiten(filtered):
    channels, length = filtered.shape
    pieces = filtered.reshape(channels, length // NF, NF)
    segment_rows = jnp.concatenate([pieces[:, :-1], pieces[:, 1:]], axis=2)
    spectrum = jnp.einsum(
        "csn,nf->csf",
        segment_rows.astype(jnp.float32),
        fourier_table(),
        precision=lax.Precision.HIGHEST,
    )
    real_part = spectrum[..., :NF]
    imag_part = spectrum[..., NF:]
    powers = real_part * real_part + imag_part * imag_part
    mean_power = jnp.mean(powers, axis=-1, keepdims=True)
    whitening = 1.0 / jnp.sqrt(powers + mean_power + 1e-06)
    return jnp.concatenate([real_part * whitening, imag_part * whitening], axis=-1).astype(
        jnp.bfloat16
    )


def cross_block(own_rows, extended):
    rows, segments, columns = own_rows.shape
    own_pairs = own_rows.reshape(rows, 2 * segments, NF)
    turned = jnp.concatenate([-extended[..., NF:], extended[..., :NF]], axis=-1)
    far_pairs = jnp.stack(
        [extended.reshape(-1, 2 * segments, NF), turned.reshape(-1, 2 * segments, NF)], axis=2
    )
    step_rows = min(16, rows)
    reach = step_rows + LAGS
    results = []
    for first in range(0, rows, step_rows):
        own_part = own_pairs[first : first + step_rows]
        far_part = far_pairs[first : first + reach]
        combined = jnp.einsum(
            "cxf,dxof->cdof", own_part, far_part, preferred_element_type=jnp.float32
        )
        combined = combined.reshape(step_rows * reach, NFFT) / segments
        combined = jnp.concatenate([combined, jnp.zeros((step_rows, NFFT), jnp.float32)], axis=0)
        banded = combined.reshape(step_rows, reach + 1, NFFT)[:, :LAGS]
        results.append(banded.astype(jnp.bfloat16))
    return jnp.concatenate(results, axis=0)


def body(strain, filter_taps):
    tap_count = filter_taps.shape[0]
    regrouped = lax.all_to_all(strain, "ta", split_axis=0, concat_axis=1, tiled=True)
    filtered = decimate(
        jnp.zeros((regrouped.shape[0], tap_count), jnp.float32),
        regrouped.astype(jnp.float32),
        filter_taps,
    )
    whitened = whiten(filtered)
    block_rows, segments, columns = whitened.shape
    reach = LAGS // block_rows
    position = lax.axis_index("ta")
    extent = lax.axis_size("ta")
    pieces = []
    for offset in range(1, reach + 1):
        pieces.append(shifted(whitened, "ta", -offset))
    stacked = jnp.stack(pieces)
    beyond = from_behind(stacked, "col", -1)
    offsets_ahead = jnp.arange(1, reach + 1, dtype=jnp.int32).reshape(reach, 1, 1, 1)
    beyond_end = position + offsets_ahead >= extent
    chosen = jnp.where(beyond_end, beyond, stacked)
    ahead_rows = chosen.reshape(reach * block_rows, segments, columns)
    extended = jnp.concatenate([whitened, ahead_rows], axis=0)
    return cross_block(whitened, extended)[None]


def solution(mesh):
    return jax.shard_map(
        body,
        mesh=mesh,
        in_specs=(P("col", "ta"), P()),
        out_specs=P("col", "ta", None, None),
        check_vma=False,
    )
```

profile of v0, /device:TPU:1, one launch (start us, length us, event | category | flops | bytes accessed | tf_op | source)
XLA Modules:
  0.0 51.3 jit_solution(17561312377843437521)
XLA Ops:
  0.0 1.0 %copy.24 = bf16[512,64]{1,0:T(8,128)(2,1)S(1)} copy(bf16[512,64]{0,1:T(8,128)(2,1)} %param.2) | data formatting | bytes 131072 | tf_op args[0]
  1.0 0.8 %reshape.138 = bf16[8,2,2048]{2,1,0:T(2,128)(2,1)} reshape(bf16[8,64,64]{2,1,0:T(8,128)(2,1)S(1)} %bitcast.78) | data formatting | bytes 131072
  1.8 6.4 %all-to-all-start = ((bf16[8,2,2048]{2,1,0:T(2,128)(2,1)}), bf16[8,2,2048]{2,1,0:T(2,128)(2,1)S(1)}, u32[]{:S(2)}, u32[]{:S(2)}) async-start(bf16[8,2,2048]{2,1,0:T(2,128)(2,1)} %reshape.138), calls=%async_computation | async-start | bytes 131072 | tf_op jit(solution)/shard_map/all_to_all | solution.py:103
  8.2 0.5 %cosine_multiply_fusion = (f32[256,128]{1,0:T(8,128)S(1)}, f32[256,128]{1,0:T(8,128)S(1)}) fusion(s32[128]{0:T(128)S(1)} %iota_add_fusion, f32[256]{0:T(256)S(1)} %get-tuple-element.15, f32[256]{0:T(256)S(1)} %get-tuple-element.16), kind=kLoop, calls=%fused_computation.32 | loop fusion | flops 524288 | bytes 264704 | tf_op jit(solution)/shard_map/mul | solution.py:54
  8.7 0.7 %rev.3 = f32[64]{0:T(128)S(1)} reverse(f32[64]{0:T(128)} %param.3), dimensions={0} | reverse | bytes 512 | tf_op jit(solution)/shard_map/rev | solution.py:26
  9.6 0.2 tile.10
  10.0 3.9 %all-to-all-done = bf16[8,2,2048]{2,1,0:T(2,128)(2,1)S(1)} async-done(((bf16[8,2,2048]{2,1,0:T(2,128)(2,1)}), bf16[8,2,2048]{2,1,0:T(2,128)(2,1)S(1)}, u32[]{:S(2)}, u32[]{:S(2)}) %all-to-all-start) | async-done | bytes 65568 | tf_op jit(solution)/shard_map/all_to_all | solution.py:103
  13.9 0.1 reshape.139
  14.1 0.2 copy.25
  14.7 0.4 convolution_convert_fusion
  15.1 0.2 convolution_bitcast_fusion
  15.6 0.4 collective-permute-start.1
  16.0 1.1 %collective-permute-start = (bf16[64,1,256]{2,0,1:T(8,128)(2,1)S(1)}, bf16[64,1,256]{2,0,1:T(8,128)(2,1)S(1)}, u32[]{:S(2)}, u32[]{:S(2)}) collective-permute-start(bf16[64,1,256]{2,0,1:T(8,128)(2,1)S(1)} %maximum_convert_fusion), channel_id=1, source_target_pairs={{4,0},{8,4},{12,8},{16,12},{20,16},{24,20},{28,24},{0,28},{5,1},{9... | collective-permute-start | bytes 98312 | tf_op jit(solution)/shard_map/ppermute | solution.py:14
  17.2 1.3 %collective-permute-done.1 = bf16[64,1,256]{2,0,1:T(8,128)(2,1)S(1)} collective-permute-done((bf16[64,1,256]{2,0,1:T(8,128)(2,1)S(1)}, bf16[64,1,256]{2,0,1:T(8,128)(2,1)S(1)}, u32[]{:S(2)}, u32[]{:S(2)}) %collective-permute-start.1) | collective-permute-done | bytes 32800 | tf_op jit(solution)/shard_map/ppermute | solution.py:14
  18.4 0.4 collective-permute-done
  18.8 5.5 %collective-permute-start.2 = (bf16[2,64,1,256]{3,1,2,0:T(8,128)(2,1)S(1)}, bf16[2,64,1,256]{3,1,2,0:T(8,128)(2,1)S(1)}, u32[]{:S(2)}, u32[]{:S(2)}) collective-permute-start(bf16[2,64,1,256]{3,1,2,0:T(8,128)(2,1)S(1)} %pad_maximum_fusion.2), channel_id=1, source_target_pairs={{1,0},{2,1},{3,2},{5,4},{6,5},{7,6},{9,8},{10,9},{11,10},{13,12},{... | collective-permute-start | bytes 196616 | tf_op jit(solution)/shard_map/ppermute | solution.py:20
  24.4 0.1 copy.29
  24.6 0.8 %copy.42 = bf16[16,2,128,1]{0,1,3,2:T(2,128)(2,1)} copy(bf16[16,2,128,1]{2,1,0,3:T(2,128)(2,1)S(1)} %bitcast.86) | data formatting | bytes 16384 | tf_op jit(solution)/shard_map/slice | solution.py:89
  25.3 0.7 %copy.43 = bf16[16,2,128,1]{0,1,3,2:T(2,128)(2,1)} copy(bf16[16,2,128,1]{2,1,0,3:T(2,128)(2,1)S(1)} %bitcast.85) | data formatting | bytes 16384 | tf_op jit(solution)/shard_map/slice | solution.py:89
  26.1 0.1 copy.44
  26.2 0.8 %copy.41 = bf16[16,2,128,1]{0,1,3,2:T(2,128)(2,1)} copy(bf16[16,2,128,1]{2,1,0,3:T(2,128)(2,1)S(1)} %bitcast.83) | data formatting | bytes 16384 | tf_op jit(solution)/shard_map/slice | solution.py:89
  26.9 0.2 collective-permute-done.2
  27.4 0.1 copy.31
  27.5 0.1 copy.30
  27.7 0.4 pad_maximum_fusion
  28.0 0.9 %convert_bitcast_fusion = bf16[16,144,2,128]{1,0,2,3:T(8,128)(2,1)S(1)} fusion(bf16[16,2,128,1]{0,1,3,2:T(2,128)(2,1)S(1)} %copy.44, bf16[192,2,2,128]{0,1,2,3:T(2,128)(2,1)S(1)} %pad_maximum_fusion), kind=kOutput, calls=%fused_computation.1 | convolution fusion | flops 2949120 | bytes 1384448 | tf_op jit(solution)/shard_map/cxf,dxof->cdof/dot_general | solution.py:91
  28.9 2.5 %copy.39 = bf16[16,144,2,128]{3,2,1,0:T(2,128)(2,1)S(1)} copy(bf16[16,144,2,128]{1,0,2,3:T(8,128)(2,1)S(1)} %convert_bitcast_fusion) | data formatting | bytes 2359296 | tf_op jit(solution)/shard_map/cxf,dxof->cdof/transpose | solution.py:91
  31.4 0.2 copy.64
  31.7 0.4 reshape.131
  32.1 1.1 %slice.124 = bf16[16,128,256]{2,1,0:T(8,128)(2,1)} slice(bf16[16,145,256]{2,1,0:T(8,128)(2,1)S(1)} %reshape.131), slice={[0:16], [0:128], [0:256]} | slice | bytes 2097152 | tf_op jit(solution)/shard_map/slice | solution.py:96
  33.2 0.9 %convert_bitcast_fusion.1 = bf16[16,144,2,128]{1,0,2,3:T(8,128)(2,1)S(1)} fusion(bf16[16,2,128,1]{0,1,3,2:T(2,128)(2,1)S(1)} %copy-done.5, bf16[192,2,2,128]{0,1,2,3:T(2,128)(2,1)S(1)} %pad_maximum_fusion), kind=kOutput, calls=%fused_computation.2 | convolution fusion | flops 2949120 | bytes 1384448 | tf_op jit(solution)/shard_map/cxf,dxof->cdof/dot_general | solution.py:91
  34.1 2.5 %copy.37 = bf16[16,144,2,128]{3,2,1,0:T(2,128)(2,1)S(1)} copy(bf16[16,144,2,128]{1,0,2,3:T(8,128)(2,1)S(1)} %convert_bitcast_fusion.1) | data formatting | bytes 2359296 | tf_op jit(solution)/shard_map/cxf,dxof->cdof/transpose | solution.py:91
  36.5 0.2 copy.65
  36.8 0.4 reshape.129
  37.2 1.1 %slice.121 = bf16[16,128,256]{2,1,0:T(8,128)(2,1)} slice(bf16[16,145,256]{2,1,0:T(8,128)(2,1)S(1)} %reshape.129), slice={[0:16], [0:128], [0:256]} | slice | bytes 2097152 | tf_op jit(solution)/shard_map/slice | solution.py:96
  38.3 0.9 %convert_bitcast_fusion.2 = bf16[16,144,2,128]{1,0,2,3:T(8,128)(2,1)S(1)} fusion(bf16[16,2,128,1]{0,1,3,2:T(2,128)(2,1)S(1)} %copy-done.4, bf16[192,2,2,128]{0,1,2,3:T(2,128)(2,1)S(1)} %pad_maximum_fusion), kind=kOutput, calls=%fused_computation.3 | convolution fusion | flops 2949120 | bytes 1384448 | tf_op jit(solution)/shard_map/cxf,dxof->cdof/dot_general | solution.py:91
  39.2 2.5 %copy.35 = bf16[16,144,2,128]{3,2,1,0:T(2,128)(2,1)S(1)} copy(bf16[16,144,2,128]{1,0,2,3:T(8,128)(2,1)S(1)} %convert_bitcast_fusion.2) | data formatting | bytes 2359296 | tf_op jit(solution)/shard_map/cxf,dxof->cdof/transpose | solution.py:91
  41.7 0.2 copy.66
  41.9 0.4 reshape.127
  42.3 1.1 %slice.118 = bf16[16,128,256]{2,1,0:T(8,128)(2,1)} slice(bf16[16,145,256]{2,1,0:T(8,128)(2,1)S(1)} %reshape.127), slice={[0:16], [0:128], [0:256]} | slice | bytes 2097152 | tf_op jit(solution)/shard_map/slice | solution.py:96
  43.5 0.8 %convert_bitcast_fusion.3 = bf16[16,144,2,128]{1,0,2,3:T(8,128)(2,1)S(1)} fusion(bf16[16,2,128,1]{0,1,3,2:T(2,128)(2,1)S(1)} %copy-done.3, bf16[192,2,2,128]{0,1,2,3:T(2,128)(2,1)S(1)} %pad_maximum_fusion), kind=kOutput, calls=%fused_computation.4 | convolution fusion | flops 2949120 | bytes 1384448 | tf_op jit(solution)/shard_map/cxf,dxof->cdof/dot_general | solution.py:91
  44.2 2.5 %copy.33 = bf16[16,144,2,128]{3,2,1,0:T(2,128)(2,1)S(1)} copy(bf16[16,144,2,128]{1,0,2,3:T(8,128)(2,1)S(1)} %convert_bitcast_fusion.3) | data formatting | bytes 2359296 | tf_op jit(solution)/shard_map/cxf,dxof->cdof/transpose | solution.py:91
  46.7 0.2 copy.67
  47.0 0.4 reshape.125
  47.5 0.7 %copy-done = bf16[16,128,256]{2,1,0:T(8,128)(2,1)S(1)} copy-done((bf16[16,128,256]{2,1,0:T(8,128)(2,1)S(1)}, bf16[16,128,256]{2,1,0:T(8,128)(2,1)}, u32[]{:S(2)}) %copy-start) | copy-done | bytes 1048600
  48.2 0.5 %copy-done.1 = bf16[16,128,256]{2,1,0:T(8,128)(2,1)S(1)} copy-done((bf16[16,128,256]{2,1,0:T(8,128)(2,1)S(1)}, bf16[16,128,256]{2,1,0:T(8,128)(2,1)}, u32[]{:S(2)}) %copy-start.1) | copy-done | bytes 1048600
  48.7 0.3 copy-done.2
  49.0 2.3 %maximum_bitcast_fusion = bf16[1,64,128,256]{3,2,1,0:T(8,128)(2,1)} fusion(bf16[16,128,256]{2,1,0:T(8,128)(2,1)S(1)} %copy-done, bf16[16,128,256]{2,1,0:T(8,128)(2,1)S(1)} %copy-done.1, bf16[16,128,256]{2,1,0:T(8,128)(2,1)S(1)} %copy-done.2, bf16[16,128,256]{2,1,0:T(8,128)(2,1)S(1)} %slice.115), kind=kLoop, calls=%fused_computation | loop fusion | flops 6291456 | bytes 8388608 | tf_op jit(solution)/shard_map/broadcast_in_dim | solution.py:124
  (50 shorter events, 1.6 us)
Async XLA Ops:
  1.8 12.1 %all-to-all-start = ((bf16[8,2,2048]{2,1,0:T(2,128)(2,1)}), bf16[8,2,2048]{2,1,0:T(2,128)(2,1)S(1)}, u32[]{:S(2)}, u32[]{:S(2)}) async-start(bf16[8,2,2048]{2,1,0:T(2,128)(2,1)} %reshape.138), calls=%async_computation | async-start | bytes 131072 | tf_op jit(solution)/shard_map/all_to_all | solution.py:103
  15.6 2.8 %collective-permute-start.1 = (bf16[64,1,256]{2,0,1:T(8,128)(2,1)S(1)}, bf16[64,1,256]{2,0,1:T(8,128)(2,1)S(1)}, u32[]{:S(2)}, u32[]{:S(2)}) collective-permute-start(bf16[64,1,256]{2,0,1:T(8,128)(2,1)S(1)} %maximum_convert_fusion), channel_id=1, source_target_pairs={{8,0},{12,4},{16,8},{20,12},{24,16},{28,20},{0,24},{4,28},{9,1},{1... | collective-permute-start | bytes 98312 | tf_op jit(solution)/shard_map/ppermute | solution.py:14
  16.0 2.8 %collective-permute-start = (bf16[64,1,256]{2,0,1:T(8,128)(2,1)S(1)}, bf16[64,1,256]{2,0,1:T(8,128)(2,1)S(1)}, u32[]{:S(2)}, u32[]{:S(2)}) collective-permute-start(bf16[64,1,256]{2,0,1:T(8,128)(2,1)S(1)} %maximum_convert_fusion), channel_id=1, source_target_pairs={{4,0},{8,4},{12,8},{16,12},{20,16},{24,20},{28,24},{0,28},{5,1},{9... | collective-permute-start | bytes 98312 | tf_op jit(solution)/shard_map/ppermute | solution.py:14
  18.8 8.4 %collective-permute-start.2 = (bf16[2,64,1,256]{3,1,2,0:T(8,128)(2,1)S(1)}, bf16[2,64,1,256]{3,1,2,0:T(8,128)(2,1)S(1)}, u32[]{:S(2)}, u32[]{:S(2)}) collective-permute-start(bf16[2,64,1,256]{3,1,2,0:T(8,128)(2,1)S(1)} %pad_maximum_fusion.2), channel_id=1, source_target_pairs={{1,0},{2,1},{3,2},{5,4},{6,5},{7,6},{9,8},{10,9},{11,10},{13,12},{... | collective-permute-start | bytes 196616 | tf_op jit(solution)/shard_map/ppermute | solution.py:20
  32.1 1.1 %copy-start.5 = (bf16[16,2,128,1]{0,1,3,2:T(2,128)(2,1)S(1)}, bf16[16,2,128,1]{0,1,3,2:T(2,128)(2,1)}, u32[]{:S(2)}) copy-start(bf16[16,2,128,1]{0,1,3,2:T(2,128)(2,1)} %copy.43) | copy-start | bytes 24580
  37.2 1.1 %copy-start.4 = (bf16[16,2,128,1]{0,1,3,2:T(2,128)(2,1)S(1)}, bf16[16,2,128,1]{0,1,3,2:T(2,128)(2,1)}, u32[]{:S(2)}) copy-start(bf16[16,2,128,1]{0,1,3,2:T(2,128)(2,1)} %copy.42) | copy-start | bytes 24580
  41.9 1.6 %copy-start.3 = (bf16[16,2,128,1]{0,1,3,2:T(2,128)(2,1)S(1)}, bf16[16,2,128,1]{0,1,3,2:T(2,128)(2,1)}, u32[]{:S(2)}) copy-start(bf16[16,2,128,1]{0,1,3,2:T(2,128)(2,1)} %copy.41) | copy-start | bytes 24580
  46.9 1.2 %copy-start = (bf16[16,128,256]{2,1,0:T(8,128)(2,1)S(1)}, bf16[16,128,256]{2,1,0:T(8,128)(2,1)}, u32[]{:S(2)}) copy-start(bf16[16,128,256]{2,1,0:T(8,128)(2,1)} %slice.124) | copy-start | bytes 3145732
  47.4 1.3 %copy-start.1 = (bf16[16,128,256]{2,1,0:T(8,128)(2,1)S(1)}, bf16[16,128,256]{2,1,0:T(8,128)(2,1)}, u32[]{:S(2)}) copy-start(bf16[16,128,256]{2,1,0:T(8,128)(2,1)} %slice.121) | copy-start | bytes 3145732
  47.4 1.6 %copy-start.2 = (bf16[16,128,256]{2,1,0:T(8,128)(2,1)S(1)}, bf16[16,128,256]{2,1,0:T(8,128)(2,1)}, u32[]{:S(2)}) copy-start(bf16[16,128,256]{2,1,0:T(8,128)(2,1)} %slice.118) | copy-start | bytes 3145732
where the time goes:
time: 51.6 us; the launch traced here: 51.3 us
  local copies, waits for them, and re-layouts  23.8 us (46%)
  starting transfers between devices  13.5 us (26%)
  waiting for transfers between devices  5.81 us (11%)
  matrix products  4.04 us (8%)
  other arithmetic  3.7 us (7%)
    transpose x4, local copies, waits for them, and re-layouts, cross_block(): jnp.einsum('cxf,dxof->cdof', own_part, far_part, preferred_element_type=j...  9.84 us
    all_to_all x1, starting transfers between devices, body(): lax.all_to_all(strain, 'ta', split_axis=0, concat_axis=1, tiled=True)  6.38 us
    ppermute x1, starting transfers between devices, from_behind(): return lax.ppermute(block, axis, route)  5.55 us
    unnamed x21, local copies, waits for them, and re-layouts  4.04 us
    all_to_all x1, waiting for transfers between devices, body(): lax.all_to_all(strain, 'ta', split_axis=0, concat_axis=1, tiled=True)  3.94 us
    dot_general x4, matrix products, cross_block(): jnp.einsum('cxf,dxof->cdof', own_part, far_part, preferred_element_type=j...  3.4 us
    slice x4, local copies, waits for them, and re-layouts, cross_block(): banded = combined.reshape(step_rows, reach + 1, NFFT)[:, :LAGS]  3.38 us
    slice x9, local copies, waits for them, and re-layouts, cross_block(): own_part = own_pairs[first:first + step_rows]  2.43 us
  transfers between devices with their start and end apart: 4, of which 4 were waited for; matrix products, arithmetic and copies ran while one was open for 8% of the time, Pallas kernels for 0%

commit v1 on v0

--- a/solution.py
+++ b/solution.py
@@ -100,7 +100,10 @@
 
 def body(strain, filter_taps):
     tap_count = filter_taps.shape[0]
-    regrouped = lax.all_to_all(strain, "ta", split_axis=0, concat_axis=1, tiled=True)
+    regrouped = jnp.concatenate(
+        lax.all_to_all(jnp.stack(jnp.split(strain, lax.axis_size("ta"), axis=0)), "ta", 0, 0),
+        axis=1,
+    )
     filtered = decimate(
         jnp.zeros((regrouped.shape[0], tap_count), jnp.float32),
         regrouped.astype(jnp.float32),

time: 51.6 us -> 56.9 us (1.10)
  local copies, waits for them, and re-layouts: 23.8 us -> 28.8 us
    unnamed x21 -> x27, local copies, waits for them, and re-layouts: 4.04 us -> 8.37 us
    another operation x0 -> x1, local copies, waits for them, and re-layouts: none -> 0.8 us  [body(): jnp.stack(jnp.split(strain, lax.axis_size('ta'), axis=0))]
where the time goes in v1:
time: 56.9 us; the launch traced here: 56.2 us
  local copies, waits for them, and re-layouts  28.8 us (51%)
  starting transfers between devices  13.5 us (24%)
  waiting for transfers between devices  5.81 us (10%)
  matrix products  4.04 us (7%)
  other arithmetic  3.7 us (7%)
    transpose x4, local copies, waits for them, and re-layouts, cross_block(): jnp.einsum('cxf,dxof->cdof', own_part, far_part, preferred_element_type=j...  9.84 us
    unnamed x27, local copies, waits for them, and re-layouts  8.37 us
    all_to_all x1, starting transfers between devices, body(): lax.all_to_all(jnp.stack(jnp.split(strain, lax.axis_size('ta'), axis=0)),...  6.38 us
    ppermute x1, starting transfers between devices, from_behind(): return lax.ppermute(block, axis, route)  5.55 us
    all_to_all x1, waiting for transfers between devices, body(): lax.all_to_all(jnp.stack(jnp.split(strain, lax.axis_size('ta'), axis=0)),...  3.94 us
    dot_general x4, matrix products, cross_block(): jnp.einsum('cxf,dxof->cdof', own_part, far_part, preferred_element_type=j...  3.4 us
    slice x4, local copies, waits for them, and re-layouts, cross_block(): banded = combined.reshape(step_rows, reach + 1, NFFT)[:, :LAGS]  3.38 us
    slice x9, local copies, waits for them, and re-layouts, cross_block(): own_part = own_pairs[first:first + step_rows]  2.43 us
  transfers between devices with their start and end apart: 4, of which 4 were waited for; matrix products, arithmetic and copies ran while one was open for 8% of the time, Pallas kernels for 0%

profile of v1, /device:TPU:1, one launch (start us, length us, event | category | flops | bytes accessed | tf_op | source)
XLA Modules:
  0.0 56.2 jit_solution(14212993251908456417)
XLA Ops:
  0.0 0.7 %constant_dynamic-update-slice_fusion.7 = bf16[8,64,64]{1,2,0:T(8,128)(2,1)S(1)} fusion(bf16[512,64]{0,1:T(8,128)(2,1)} %param.2), kind=kLoop, calls=%fused_computation.58 | loop fusion | bytes 24576
  0.7 0.8 %constant_dynamic-update-slice_fusion.6 = bf16[8,64,64]{1,2,0:T(8,128)(2,1)S(1)} fusion(bf16[8,64,64]{1,2,0:T(8,128)(2,1)S(1)} %constant_dynamic-update-slice_fusion.7, bf16[512,64]{0,1:T(8,128)(2,1)} %param.2), kind=kLoop, calls=%fused_computation.57 | loop fusion | bytes 24576
  1.5 0.7 %constant_dynamic-update-slice_fusion.5 = bf16[8,64,64]{1,2,0:T(8,128)(2,1)S(1)} fusion(bf16[8,64,64]{1,2,0:T(8,128)(2,1)S(1)} %constant_dynamic-update-slice_fusion.6, bf16[512,64]{0,1:T(8,128)(2,1)} %param.2), kind=kLoop, calls=%fused_computation.56 | loop fusion | bytes 24576
  2.2 0.8 %constant_dynamic-update-slice_fusion.4 = bf16[8,64,64]{1,2,0:T(8,128)(2,1)S(1)} fusion(bf16[8,64,64]{1,2,0:T(8,128)(2,1)S(1)} %constant_dynamic-update-slice_fusion.5, bf16[512,64]{0,1:T(8,128)(2,1)} %param.2), kind=kLoop, calls=%fused_computation.55 | loop fusion | bytes 24576
  3.0 0.7 %constant_dynamic-update-slice_fusion.3 = bf16[8,64,64]{1,2,0:T(8,128)(2,1)S(1)} fusion(bf16[8,64,64]{1,2,0:T(8,128)(2,1)S(1)} %constant_dynamic-update-slice_fusion.4, bf16[512,64]{0,1:T(8,128)(2,1)} %param.2), kind=kLoop, calls=%fused_computation.54 | loop fusion | bytes 24576
  3.8 0.8 %constant_dynamic-update-slice_fusion.2 = bf16[8,64,64]{1,2,0:T(8,128)(2,1)S(1)} fusion(bf16[8,64,64]{1,2,0:T(8,128)(2,1)S(1)} %constant_dynamic-update-slice_fusion.3, bf16[512,64]{0,1:T(8,128)(2,1)} %param.2), kind=kLoop, calls=%fused_computation.53 | loop fusion | bytes 24576
  4.6 0.7 %constant_dynamic-update-slice_fusion.1 = bf16[8,64,64]{1,2,0:T(8,128)(2,1)S(1)} fusion(bf16[8,64,64]{1,2,0:T(8,128)(2,1)S(1)} %constant_dynamic-update-slice_fusion.2, bf16[512,64]{0,1:T(8,128)(2,1)} %param.2), kind=kLoop, calls=%fused_computation.52 | loop fusion | bytes 24576
  5.3 0.8 %constant_dynamic-update-slice_fusion = bf16[8,64,64]{1,2,0:T(8,128)(2,1)S(1)} fusion(bf16[8,64,64]{1,2,0:T(8,128)(2,1)S(1)} %constant_dynamic-update-slice_fusion.1, bf16[512,64]{0,1:T(8,128)(2,1)} %param.2), kind=kLoop, calls=%fused_computation.51 | loop fusion | bytes 24576 | tf_op jit(solution)/shard_map/stack | solution.py:104
  6.1 0.8 %reshape.137 = bf16[8,2,2048]{2,1,0:T(2,128)(2,1)} reshape(bf16[8,64,64]{2,1,0:T(8,128)(2,1)S(1)} %bitcast.98) | data formatting | bytes 131072
  6.9 6.4 %all-to-all-start = ((bf16[8,2,2048]{2,1,0:T(2,128)(2,1)}), bf16[8,2,2048]{2,1,0:T(2,128)(2,1)S(1)}, u32[]{:S(2)}, u32[]{:S(2)}) async-start(bf16[8,2,2048]{2,1,0:T(2,128)(2,1)} %reshape.137), calls=%async_computation | async-start | bytes 131072 | tf_op jit(solution)/shard_map/all_to_all | solution.py:104
  13.3 0.5 cosine_multiply_fusion
  13.9 0.7 %rev.3 = f32[64]{0:T(128)S(1)} reverse(f32[64]{0:T(128)} %param.3), dimensions={0} | reverse | bytes 512 | tf_op jit(solution)/shard_map/rev | solution.py:26
  14.7 0.2 tile.10
  15.1 3.9 %all-to-all-done = bf16[8,2,2048]{2,1,0:T(2,128)(2,1)S(1)} async-done(((bf16[8,2,2048]{2,1,0:T(2,128)(2,1)}), bf16[8,2,2048]{2,1,0:T(2,128)(2,1)S(1)}, u32[]{:S(2)}, u32[]{:S(2)}) %all-to-all-start) | async-done | bytes 65568 | tf_op jit(solution)/shard_map/all_to_all | solution.py:104
  19.7 0.4 convolution_convert_fusion
  20.1 0.2 convolution_bitcast_fusion
  20.6 0.4 collective-permute-start.1
  21.0 1.1 %collective-permute-start = (bf16[64,1,256]{2,0,1:T(8,128)(2,1)S(1)}, bf16[64,1,256]{2,0,1:T(8,128)(2,1)S(1)}, u32[]{:S(2)}, u32[]{:S(2)}) collective-permute-start(bf16[64,1,256]{2,0,1:T(8,128)(2,1)S(1)} %maximum_convert_fusion), channel_id=1, source_target_pairs={{4,0},{8,4},{12,8},{16,12},{20,16},{24,20},{28,24},{0,28},{5,1},{9... | collective-permute-start | bytes 98312 | tf_op jit(solution)/shard_map/ppermute | solution.py:14
  22.1 1.3 %collective-permute-done.1 = bf16[64,1,256]{2,0,1:T(8,128)(2,1)S(1)} collective-permute-done((bf16[64,1,256]{2,0,1:T(8,128)(2,1)S(1)}, bf16[64,1,256]{2,0,1:T(8,128)(2,1)S(1)}, u32[]{:S(2)}, u32[]{:S(2)}) %collective-permute-start.1) | collective-permute-done | bytes 32800 | tf_op jit(solution)/shard_map/ppermute | solution.py:14
  23.4 0.4 collective-permute-done
  23.8 5.5 %collective-permute-start.2 = (bf16[2,64,1,256]{3,1,2,0:T(8,128)(2,1)S(1)}, bf16[2,64,1,256]{3,1,2,0:T(8,128)(2,1)S(1)}, u32[]{:S(2)}, u32[]{:S(2)}) collective-permute-start(bf16[2,64,1,256]{3,1,2,0:T(8,128)(2,1)S(1)} %pad_maximum_fusion.2), channel_id=1, source_target_pairs={{1,0},{2,1},{3,2},{5,4},{6,5},{7,6},{9,8},{10,9},{11,10},{13,12},{... | collective-permute-start | bytes 196616 | tf_op jit(solution)/shard_map/ppermute | solution.py:20
  29.5 0.8 %copy.26 = bf16[16,2,128,1]{0,1,3,2:T(2,128)(2,1)} copy(bf16[16,2,128,1]{2,1,0,3:T(2,128)(2,1)S(1)} %bitcast.106) | data formatting | bytes 16384 | tf_op jit(solution)/shard_map/slice | solution.py:89
  30.3 0.7 %copy.27 = bf16[16,2,128,1]{0,1,3,2:T(2,128)(2,1)} copy(bf16[16,2,128,1]{2,1,0,3:T(2,128)(2,1)S(1)} %bitcast.105) | data formatting | bytes 16384 | tf_op jit(solution)/shard_map/slice | solution.py:89
  31.2 0.8 %copy.25 = bf16[16,2,128,1]{0,1,3,2:T(2,128)(2,1)} copy(bf16[16,2,128,1]{2,1,0,3:T(2,128)(2,1)S(1)} %bitcast.103) | data formatting | bytes 16384 | tf_op jit(solution)/shard_map/slice | solution.py:89
  31.9 0.2 collective-permute-done.2
  32.6 0.4 pad_maximum_fusion
  33.0 0.9 %convert_bitcast_fusion = bf16[16,144,2,128]{1,0,2,3:T(8,128)(2,1)S(1)} fusion(bf16[16,2,128,1]{0,1,3,2:T(2,128)(2,1)S(1)} %copy.28, bf16[192,2,2,128]{0,1,2,3:T(2,128)(2,1)S(1)} %pad_maximum_fusion), kind=kOutput, calls=%fused_computation.1 | convolution fusion | flops 2949120 | bytes 1384448 | tf_op jit(solution)/shard_map/cxf,dxof->cdof/dot_general | solution.py:91
  33.9 2.5 %copy.23 = bf16[16,144,2,128]{3,2,1,0:T(2,128)(2,1)S(1)} copy(bf16[16,144,2,128]{1,0,2,3:T(8,128)(2,1)S(1)} %convert_bitcast_fusion) | data formatting | bytes 2359296 | tf_op jit(solution)/shard_map/cxf,dxof->cdof/transpose | solution.py:91
  36.4 0.2 copy.48
  36.6 0.4 reshape.130
  37.1 1.1 %slice.124 = bf16[16,128,256]{2,1,0:T(8,128)(2,1)} slice(bf16[16,145,256]{2,1,0:T(8,128)(2,1)S(1)} %reshape.130), slice={[0:16], [0:128], [0:256]} | slice | bytes 2097152 | tf_op jit(solution)/shard_map/slice | solution.py:96
  38.1 0.9 %convert_bitcast_fusion.1 = bf16[16,144,2,128]{1,0,2,3:T(8,128)(2,1)S(1)} fusion(bf16[16,2,128,1]{0,1,3,2:T(2,128)(2,1)S(1)} %copy-done.5, bf16[192,2,2,128]{0,1,2,3:T(2,128)(2,1)S(1)} %pad_maximum_fusion), kind=kOutput, calls=%fused_computation.2 | convolution fusion | flops 2949120 | bytes 1384448 | tf_op jit(solution)/shard_map/cxf,dxof->cdof/dot_general | solution.py:91
  39.0 2.5 %copy.21 = bf16[16,144,2,128]{3,2,1,0:T(2,128)(2,1)S(1)} copy(bf16[16,144,2,128]{1,0,2,3:T(8,128)(2,1)S(1)} %convert_bitcast_fusion.1) | data formatting | bytes 2359296 | tf_op jit(solution)/shard_map/cxf,dxof->cdof/transpose | solution.py:91
  41.5 0.2 copy.49
  41.7 0.4 reshape.128
  42.2 1.1 %slice.121 = bf16[16,128,256]{2,1,0:T(8,128)(2,1)} slice(bf16[16,145,256]{2,1,0:T(8,128)(2,1)S(1)} %reshape.128), slice={[0:16], [0:128], [0:256]} | slice | bytes 2097152 | tf_op jit(solution)/shard_map/slice | solution.py:96
  43.3 0.9 %convert_bitcast_fusion.2 = bf16[16,144,2,128]{1,0,2,3:T(8,128)(2,1)S(1)} fusion(bf16[16,2,128,1]{0,1,3,2:T(2,128)(2,1)S(1)} %copy-done.4, bf16[192,2,2,128]{0,1,2,3:T(2,128)(2,1)S(1)} %pad_maximum_fusion), kind=kOutput, calls=%fused_computation.3 | convolution fusion | flops 2949120 | bytes 1384448 | tf_op jit(solution)/shard_map/cxf,dxof->cdof/dot_general | solution.py:91
  44.2 2.5 %copy.19 = bf16[16,144,2,128]{3,2,1,0:T(2,128)(2,1)S(1)} copy(bf16[16,144,2,128]{1,0,2,3:T(8,128)(2,1)S(1)} %convert_bitcast_fusion.2) | data formatting | bytes 2359296 | tf_op jit(solution)/shard_map/cxf,dxof->cdof/transpose | solution.py:91
  46.6 0.2 copy.50
  46.9 0.4 reshape.126
  47.3 1.1 %slice.118 = bf16[16,128,256]{2,1,0:T(8,128)(2,1)} slice(bf16[16,145,256]{2,1,0:T(8,128)(2,1)S(1)} %reshape.126), slice={[0:16], [0:128], [0:256]} | slice | bytes 2097152 | tf_op jit(solution)/shard_map/slice | solution.py:96
  48.4 0.8 %convert_bitcast_fusion.3 = bf16[16,144,2,128]{1,0,2,3:T(8,128)(2,1)S(1)} fusion(bf16[16,2,128,1]{0,1,3,2:T(2,128)(2,1)S(1)} %copy-done.3, bf16[192,2,2,128]{0,1,2,3:T(2,128)(2,1)S(1)} %pad_maximum_fusion), kind=kOutput, calls=%fused_computation.4 | convolution fusion | flops 2949120 | bytes 1384448 | tf_op jit(solution)/shard_map/cxf,dxof->cdof/dot_general | solution.py:91
  49.2 2.5 %copy.17 = bf16[16,144,2,128]{3,2,1,0:T(2,128)(2,1)S(1)} copy(bf16[16,144,2,128]{1,0,2,3:T(8,128)(2,1)S(1)} %convert_bitcast_fusion.3) | data formatting | bytes 2359296 | tf_op jit(solution)/shard_map/cxf,dxof->cdof/transpose | solution.py:91
  51.9 0.4 reshape.124
  52.5 0.7 %copy-done = bf16[16,128,256]{2,1,0:T(8,128)(2,1)S(1)} copy-done((bf16[16,128,256]{2,1,0:T(8,128)(2,1)S(1)}, bf16[16,128,256]{2,1,0:T(8,128)(2,1)}, u32[]{:S(2)}) %copy-start) | copy-done | bytes 1048600
  53.1 0.5 copy-done.1
  53.7 0.3 copy-done.2
  54.0 2.3 %maximum_bitcast_fusion = bf16[1,64,128,256]{3,2,1,0:T(8,128)(2,1)} fusion(bf16[16,128,256]{2,1,0:T(8,128)(2,1)S(1)} %copy-done, bf16[16,128,256]{2,1,0:T(8,128)(2,1)S(1)} %copy-done.1, bf16[16,128,256]{2,1,0:T(8,128)(2,1)S(1)} %copy-done.2, bf16[16,128,256]{2,1,0:T(8,128)(2,1)S(1)} %slice.115), kind=kLoop, calls=%fused_computation | loop fusion | flops 6291456 | bytes 8388608 | tf_op jit(solution)/shard_map/broadcast_in_dim | solution.py:127
  (56 shorter events, 2.4 us)
Async XLA Ops:
  6.9 12.1 %all-to-all-start = ((bf16[8,2,2048]{2,1,0:T(2,128)(2,1)}), bf16[8,2,2048]{2,1,0:T(2,128)(2,1)S(1)}, u32[]{:S(2)}, u32[]{:S(2)}) async-start(bf16[8,2,2048]{2,1,0:T(2,128)(2,1)} %reshape.137), calls=%async_computation | async-start | bytes 131072 | tf_op jit(solution)/shard_map/all_to_all | solution.py:104
  20.6 2.8 %collective-permute-start.1 = (bf16[64,1,256]{2,0,1:T(8,128)(2,1)S(1)}, bf16[64,1,256]{2,0,1:T(8,128)(2,1)S(1)}, u32[]{:S(2)}, u32[]{:S(2)}) collective-permute-start(bf16[64,1,256]{2,0,1:T(8,128)(2,1)S(1)} %maximum_convert_fusion), channel_id=1, source_target_pairs={{8,0},{12,4},{16,8},{20,12},{24,16},{28,20},{0,24},{4,28},{9,1},{1... | collective-permute-start | bytes 98312 | tf_op jit(solution)/shard_map/ppermute | solution.py:14
  21.0 2.8 %collective-permute-start = (bf16[64,1,256]{2,0,1:T(8,128)(2,1)S(1)}, bf16[64,1,256]{2,0,1:T(8,128)(2,1)S(1)}, u32[]{:S(2)}, u32[]{:S(2)}) collective-permute-start(bf16[64,1,256]{2,0,1:T(8,128)(2,1)S(1)} %maximum_convert_fusion), channel_id=1, source_target_pairs={{4,0},{8,4},{12,8},{16,12},{20,16},{24,20},{28,24},{0,28},{5,1},{9... | collective-permute-start | bytes 98312 | tf_op jit(solution)/shard_map/ppermute | solution.py:14
  23.8 8.4 %collective-permute-start.2 = (bf16[2,64,1,256]{3,1,2,0:T(8,128)(2,1)S(1)}, bf16[2,64,1,256]{3,1,2,0:T(8,128)(2,1)S(1)}, u32[]{:S(2)}, u32[]{:S(2)}) collective-permute-start(bf16[2,64,1,256]{3,1,2,0:T(8,128)(2,1)S(1)} %pad_maximum_fusion.2), channel_id=1, source_target_pairs={{1,0},{2,1},{3,2},{5,4},{6,5},{7,6},{9,8},{10,9},{11,10},{13,12},{... | collective-permute-start | bytes 196616 | tf_op jit(solution)/shard_map/ppermute | solution.py:20
  37.0 1.1 %copy-start.5 = (bf16[16,2,128,1]{0,1,3,2:T(2,128)(2,1)S(1)}, bf16[16,2,128,1]{0,1,3,2:T(2,128)(2,1)}, u32[]{:S(2)}) copy-start(bf16[16,2,128,1]{0,1,3,2:T(2,128)(2,1)} %copy.27) | copy-start | bytes 24580
  42.2 1.1 %copy-start.4 = (bf16[16,2,128,1]{0,1,3,2:T(2,128)(2,1)S(1)}, bf16[16,2,128,1]{0,1,3,2:T(2,128)(2,1)}, u32[]{:S(2)}) copy-start(bf16[16,2,128,1]{0,1,3,2:T(2,128)(2,1)} %copy.26) | copy-start | bytes 24580
  46.9 1.6 %copy-start.3 = (bf16[16,2,128,1]{0,1,3,2:T(2,128)(2,1)S(1)}, bf16[16,2,128,1]{0,1,3,2:T(2,128)(2,1)}, u32[]{:S(2)}) copy-start(bf16[16,2,128,1]{0,1,3,2:T(2,128)(2,1)} %copy.25) | copy-start | bytes 24580
  51.9 1.2 %copy-start = (bf16[16,128,256]{2,1,0:T(8,128)(2,1)S(1)}, bf16[16,128,256]{2,1,0:T(8,128)(2,1)}, u32[]{:S(2)}) copy-start(bf16[16,128,256]{2,1,0:T(8,128)(2,1)} %slice.124) | copy-start | bytes 3145732
  52.4 1.3 %copy-start.1 = (bf16[16,128,256]{2,1,0:T(8,128)(2,1)S(1)}, bf16[16,128,256]{2,1,0:T(8,128)(2,1)}, u32[]{:S(2)}) copy-start(bf16[16,128,256]{2,1,0:T(8,128)(2,1)} %slice.121) | copy-start | bytes 3145732
  52.4 1.6 %copy-start.2 = (bf16[16,128,256]{2,1,0:T(8,128)(2,1)S(1)}, bf16[16,128,256]{2,1,0:T(8,128)(2,1)}, u32[]{:S(2)}) copy-start(bf16[16,128,256]{2,1,0:T(8,128)(2,1)} %slice.118) | copy-start | bytes 3145732
